TPU v7x, 256 devices: a whole 4x4x8 slice. The times are simulated.
256 devices in a mesh: row: 8 (over z), col: 32 (over y, x, core).
Axes of the slice: x: 4, y: 4, z: 8, core: 2. Of those that a mesh axis runs over, the one named last changes fastest.
Arguments:
- tokens: bfloat16 [512, 8192], P('col', 'row'), may hold values from -6 to 6
- cotangent: bfloat16 [512, 8192], P('col', 'row'), may hold values from -6 to 6
- w_gate: bfloat16 [8192, 16384], P('row', 'col'), may hold values from -0.09375 to 0.09375
- w_up: bfloat16 [8192, 16384], P('row', 'col'), may hold values from -0.09375 to 0.09375
- w_down: bfloat16 [16384, 8192], P('col', 'row'), may hold values from -0.0625 to 0.0625
- order_gate: int32 [2048], replicated, may hold values from 0 to 2047, each once
- order_up: int32 [2048], replicated, may hold values from 0 to 2047, each once
- order_down: int32 [2048], replicated, may hold values from 0 to 2047, each once
Outputs:
- output: bfloat16 [512, 8192], P('col', 'row')
- input_grad: bfloat16 [512, 8192], P('col', 'row')
- gate_weight_grad: float32 [8192, 16384], P('row', 'col')
- up_weight_grad: float32 [8192, 16384], P('row', 'col')
- down_weight_grad: float32 [16384, 8192], P('col', 'row')
Inputs may be any that keep to these rules, and one draw needn't show every extreme that they name: `order_gate`: each of the 2048 block numbers appears exactly once. `order_up`: each of the 2048 block numbers appears exactly once. `order_down`: each of the 2048 block numbers appears exactly once.
All inputs are finite; a program needn't handle non-finite values.
Results may differ from a plain program's by a relative error of at most 0.0049.
Values may be sent and summed in bfloat16 or wider, within the bound.
No kernel may reach another device: no remote copies, remote signals or barrier semaphores. Data moves between devices by JAX's collectives and lax.ppermute only.
A program may use at most 64 MiB of HBM per device.

v0:
```python
import jax
import jax.numpy as jnp
from jax import lax
from jax.sharding import PartitionSpec as P

BLOCK = 256


def kept_table(order, row_first, col_first, row_count, col_count, stride):
    kept_count = order.shape[0] // 2
    row_ids = row_first + jnp.arange(row_count, dtype=jnp.int32)
    col_ids = col_first + jnp.arange(col_count, dtype=jnp.int32)
    block_ids = row_ids[:, None] * stride + col_ids[None, :]
    return jnp.any(block_ids[:, :, None] == order[:kept_count][None, None, :], axis=2)


def expand_mask(kept_mask):
    row_count, col_count = kept_mask.shape
    spread = jnp.broadcast_to(kept_mask[:, None, :, None], (row_count, BLOCK, col_count, BLOCK))
    return spread.reshape(row_count * BLOCK, col_count * BLOCK)


def dense_apply(left_operand, right_operand, kept_mask, product_kind):
    full_mask = expand_mask(kept_mask)
    if product_kind == "forward":
        masked = right_operand * full_mask.astype(right_operand.dtype)
        return jnp.dot(left_operand, masked, preferred_element_type=jnp.float32)
    if product_kind == "transposed":
        masked = right_operand * full_mask.astype(right_operand.dtype)
        return lax.dot_general(
            left_operand, masked, (((1,), (1,)), ((), ())), preferred_element_type=jnp.float32
        )
    product = lax.dot_general(
        left_operand, right_operand, (((0,), (0,)), ((), ())), preferred_element_type=jnp.float32
    )
    return product * full_mask.astype(jnp.float32)


def apply_blocks(left_operand, right_operand, kept_mask, product_kind):
    return dense_apply(left_operand, right_operand, kept_mask, product_kind)


def a2a_scatter_sum(parts, axis_name):
    count = lax.axis_size(axis_name)
    pieces = parts.reshape((count, parts.shape[0] // count) + parts.shape[1:])
    return lax.all_to_all(pieces, axis_name, 0, 0, tiled=True).sum(axis=0)


def a2a_gather(block, axis_name):
    count = lax.axis_size(axis_name)
    spread = jnp.broadcast_to(block[None], (count,) + block.shape)
    gathered = lax.all_to_all(spread, axis_name, 0, 0, tiled=True)
    return gathered.reshape((count * block.shape[0],) + block.shape[1:])


def on_device(tokens, cotangent, w_gate, w_up, w_down, order_gate, order_up, order_down):
    rows_here = w_gate.shape[0] // BLOCK
    cols_here = w_gate.shape[1] // BLOCK
    row_start = lax.axis_index("row") * rows_here
    col_start = lax.axis_index("col") * cols_here
    width_blocks = rows_here * lax.axis_size("row")
    hidden_blocks = cols_here * lax.axis_size("col")
    hidden_here = w_gate.shape[1]
    keep_gate = kept_table(order_gate, row_start, col_start, rows_here, cols_here, hidden_blocks)
    keep_up = kept_table(order_up, row_start, col_start, rows_here, cols_here, hidden_blocks)
    keep_down = kept_table(order_down, col_start, row_start, cols_here, rows_here, width_blocks)
    cotangent_all = lax.all_gather(cotangent, "col", axis=0, tiled=True)
    tokens_all = a2a_gather(tokens, "col")
    gate_term = apply_blocks(tokens_all, w_gate, keep_gate, "forward")
    up_term = apply_blocks(tokens_all, w_up, keep_up, "forward")
    both = a2a_scatter_sum(jnp.concatenate([gate_term, up_term], axis=1), "row")
    gate, up = (both[:, :hidden_here], both[:, hidden_here:])
    hidden_term = apply_blocks(cotangent_all, w_down, keep_down, "transposed")
    hidden_grad = a2a_scatter_sum(hidden_term, "row")
    sigmoid_gate = jax.nn.sigmoid(gate)
    activation = gate * sigmoid_gate
    hidden = (activation * up).astype(jnp.bfloat16)
    hidden_all = a2a_gather(hidden, "row")
    output_term = apply_blocks(hidden_all, w_down, keep_down, "forward")
    output = lax.psum_scatter(output_term, "col", scatter_dimension=0, tiled=True).astype(
        jnp.bfloat16
    )
    gate_grad = (hidden_grad * up * sigmoid_gate * (1.0 + gate * (1.0 - sigmoid_gate))).astype(
        jnp.bfloat16
    )
    up_grad = (hidden_grad * activation).astype(jnp.bfloat16)
    grads_all = a2a_gather(jnp.concatenate([gate_grad, up_grad], axis=1), "row")
    gate_grad_all, up_grad_all = (grads_all[:, :hidden_here], grads_all[:, hidden_here:])
    down_weight_grad = apply_blocks(hidden_all, cotangent_all, keep_down, "weights")
    gate_weight_grad = apply_blocks(tokens_all, gate_grad_all, keep_gate, "weights")
    up_weight_grad = apply_blocks(tokens_all, up_grad_all, keep_up, "weights")
    through_gate = apply_blocks(gate_grad_all, w_gate, keep_gate, "transposed")
    through_up = apply_blocks(up_grad_all, w_up, keep_up, "transposed")
    input_grad = a2a_scatter_sum(through_gate + through_up, "col")
    return (
        output,
        input_grad.astype(jnp.bfloat16),
        gate_weight_grad,
        up_weight_grad,
        down_weight_grad,
    )


def solution(mesh):
    placed = (
        P("col", "row"),
        P("col", "row"),
        P("row", "col"),
        P("row", "col"),
        P("col", "row"),
        P(),
        P(),
        P(),
    )
    return jax.shard_map(
        on_device,
        mesh=mesh,
        in_specs=placed,
        out_specs=(
            P("col", "row"),
            P("col", "row"),
            P("row", "col"),
            P("row", "col"),
            P("col", "row"),
        ),
        check_vma=False,
    )
```

profile of v0, /device:TPU:2, one launch (start us, length us, event | category | flops | bytes accessed | tf_op | source)
XLA Modules:
  0.0 282.0 jit_solution(4696219631229832951)
XLA Ops:
  7.9 1.9 broadcast_in_dim.13
  9.8 7.8 %all-to-all-start = ((bf16[32,16,1024]{2,1,0:T(8,128)(2,1)}), bf16[32,16,1024]{2,1,0:T(8,128)(2,1)S(1)}, u32[]{:S(2)}, u32[]{:S(2)}) async-start(bf16[32,16,1024]{2,1,0:T(8,128)(2,1)} %broadcast_in_dim.13), calls=%async_computation | async-start | bytes 2097152 | tf_op jit(solution)/shard_map/all_to_all | solution.py:52
  18.5 44.1 %all-gather.2.cloned.1.call-done = bf16[512,1024]{1,0:T(8,128)(2,1)} async-done(((bf16[16,1024]{1,0:T(8,128)(2,1)}), bf16[512,1024]{1,0:T(8,128)(2,1)}) %all-gather.2.cloned.1.call-update) | async-done | bytes 1048592 | tf_op jit(solution)/shard_map/all_gather | solution.py:67
  62.5 2.9 %fusion = f32[512,512]{0,1:T(8,128)} fusion(bf16[512,1024]{1,0:T(8,128)(2,1)} %all-gather.2.cloned.1.call-done, pred[512,1024]{1,0:T(8,128)(4,1)S(1)} %bitcast.50, bf16[512,1024]{1,0:T(8,128)(2,1)S(1)} %copy-done.13), kind=kOutput, calls=%fused_computation.7 | convolution fusion | flops 537395200 | bytes 3670016 | tf_op jit(solution)/shard_map/dot_general | solution.py:30
  65.5 7.0 %all-to-all-start.3 = ((f32[8,64,512]{2,1,0:T(8,128)}), f32[8,64,512]{2,1,0:T(8,128)S(1)}, u32[]{:S(2)}, u32[]{:S(2)}) async-start(f32[8,64,512]{2,1,0:T(8,128)} %bitcast.57), calls=%async_computation.4 | async-start | bytes 2097152 | tf_op jit(solution)/shard_map/all_to_all | solution.py:46
  73.5 1.7 copy.23
  75.5 1.1 copy.27
  76.6 2.3 copy.22
  78.8 2.1 convolution_bitcast_fusion
  81.0 0.8 convolution_bitcast_fusion.1
  82.0 1.8 copy.24
  83.8 17.9 %all-to-all-done.3 = f32[8,64,512]{2,1,0:T(8,128)S(1)} async-done(((f32[8,64,512]{2,1,0:T(8,128)}), f32[8,64,512]{2,1,0:T(8,128)S(1)}, u32[]{:S(2)}, u32[]{:S(2)}) %all-to-all-start.3) | async-done | bytes 1048608 | tf_op jit(solution)/shard_map/all_to_all | solution.py:46
  101.7 3.6 %all-to-all-start.1 = ((f32[8,64,1024]{2,1,0:T(8,128)}), f32[8,64,1024]{2,1,0:T(8,128)S(1)}, u32[]{:S(2)}, u32[]{:S(2)}) async-start(f32[8,64,1024]{2,1,0:T(8,128)} %bitcast.37), calls=%async_computation.1 | async-start | bytes 4194304 | tf_op jit(solution)/shard_map/all_to_all | solution.py:46
  105.4 51.5 %all-to-all-done.1 = f32[8,64,1024]{2,1,0:T(8,128)S(1)} async-done(((f32[8,64,1024]{2,1,0:T(8,128)}), f32[8,64,1024]{2,1,0:T(8,128)S(1)}, u32[]{:S(2)}, u32[]{:S(2)}) %all-to-all-start.1) | async-done | bytes 2097184 | tf_op jit(solution)/shard_map/all_to_all | solution.py:46
  157.1 0.8 broadcast_in_dim.15
  158.0 3.6 %all-to-all-start.2 = ((bf16[8,64,512]{2,1,0:T(8,128)(2,1)}), bf16[8,64,512]{2,1,0:T(8,128)(2,1)S(1)}, u32[]{:S(2)}, u32[]{:S(2)}) async-start(bf16[8,64,512]{2,1,0:T(8,128)(2,1)} %broadcast_in_dim.15), calls=%async_computation.2 | async-start | bytes 1048576 | tf_op jit(solution)/shard_map/all_to_all | solution.py:52
  161.6 15.9 %all-to-all-done.2 = bf16[8,64,512]{2,1,0:T(8,128)(2,1)S(1)} async-done(((bf16[8,64,512]{2,1,0:T(8,128)(2,1)}), bf16[8,64,512]{2,1,0:T(8,128)(2,1)S(1)}, u32[]{:S(2)}, u32[]{:S(2)}) %all-to-all-start.2) | async-done | bytes 524320 | tf_op jit(solution)/shard_map/all_to_all | solution.py:52
  177.5 1.1 broadcast_in_dim.17
  178.6 3.6 %all-to-all-start.4 = ((bf16[8,64,1024]{2,1,0:T(8,128)(2,1)}), bf16[8,64,1024]{2,1,0:T(8,128)(2,1)S(1)}, u32[]{:S(2)}, u32[]{:S(2)}) async-start(bf16[8,64,1024]{2,1,0:T(8,128)(2,1)} %broadcast_in_dim.17), calls=%async_computation.5 | async-start | bytes 2097152 | tf_op jit(solution)/shard_map/all_to_all | solution.py:52
  182.2 2.0 fusion.2
  184.3 24.2 %all-to-all-done.4 = bf16[8,64,1024]{2,1,0:T(8,128)(2,1)S(1)} async-done(((bf16[8,64,1024]{2,1,0:T(8,128)(2,1)}), bf16[8,64,1024]{2,1,0:T(8,128)(2,1)S(1)}, u32[]{:S(2)}, u32[]{:S(2)}) %all-to-all-start.4) | async-done | bytes 1048608 | tf_op jit(solution)/shard_map/all_to_all | solution.py:52
  208.5 2.4 fusion.6
  210.9 2.1 convolution_add_fusion
  213.0 5.9 %all-to-all-start.5 = ((f32[32,16,1024]{2,1,0:T(8,128)}), f32[32,16,1024]{2,1,0:T(8,128)S(1)}, u32[]{:S(2)}, u32[]{:S(2)}) async-start(f32[32,16,1024]{2,1,0:T(8,128)} %bitcast.8), calls=%async_computation.6 | async-start | bytes 4194304 | tf_op jit(solution)/shard_map/all_to_all | solution.py:46
  218.9 3.4 %convolution_select_fusion = f32[512,1024]{1,0:T(8,128)} fusion(pred[512,1024]{1,0:T(8,128)(4,1)S(1)} %bitcast.52, bf16[512,512]{1,0:T(8,128)(2,1)S(1)} %bitcast.39, bf16[512,1024]{1,0:T(8,128)(2,1)} %all-gather.2.cloned.1.call-done), kind=kOutput, calls=%fused_computation.3 | convolution fusion | flops 537395200 | bytes 4194304 | tf_op jit(solution)/shard_map/dot_general | solution.py:33
  222.3 2.1 bitcast_select_fusion.1
  224.4 3.0 %copy.25 = f32[1024,512]{1,0:T(8,128)} copy(f32[1024,512]{0,1:T(8,128)} %bitcast_select_fusion.1) | data formatting | bytes 4194304
  227.3 3.5 %bitcast_select_fusion = f32[1024,512]{0,1:T(8,128)} fusion(pred[1024,512]{0,1:T(8,128)(4,1)} %bitcast.45, bf16[512,1024]{1,0:T(8,128)(2,1)} %bitcast.54, bf16[512,1024]{1,0:T(8,128)(2,1)S(1)} %bitcast.43), kind=kOutput, calls=%fused_computation.1 | convolution fusion | flops 537395200 | bytes 4194304 | tf_op jit(solution)/shard_map/dot_general | solution.py:33
  230.8 2.9 %copy.26 = f32[1024,512]{1,0:T(8,128)} copy(f32[1024,512]{0,1:T(8,128)} %bitcast_select_fusion) | data formatting | bytes 4194304
  233.7 14.9 %all-to-all-done.5 = f32[32,16,1024]{2,1,0:T(8,128)S(1)} async-done(((f32[32,16,1024]{2,1,0:T(8,128)}), f32[32,16,1024]{2,1,0:T(8,128)S(1)}, u32[]{:S(2)}, u32[]{:S(2)}) %all-to-all-start.5) | async-done | bytes 2097184 | tf_op jit(solution)/shard_map/all_to_all | solution.py:46
  249.3 24.4 %reduce-scatter.2.cloned.1.call-done = f32[16,1024]{1,0:T(8,128)} async-done(((f32[512,1024]{1,0:T(8,128)}), f32[16,1024]{1,0:T(8,128)}) %reduce-scatter.2.cloned.1.call-update) | async-done | bytes 65552 | tf_op jit(solution)/shard_map/reduce_scatter | solution.py:80
  273.7 1.5 convert_element_type.11
  (64 shorter events, 4.2 us)
Async XLA Ops:
  7.2 10.5 %slice-start = ((s32[2048]{0:T(1024)}), s32[1024]{0:T(1024)S(1)}, s32[]{:S(2)}) async-start(s32[2048]{0:T(1024)} %param.15), calls=%async_computation.9 | async-start | bytes 8192 | tf_op jit(solution)/shard_map/slice | solution.py:14
  7.2 55.4 %all-gather.2.cloned.1.call-start = ((), (), s32[]{:S(2)}) async-start(), calls=%async_computation.8 | async-start | bytes 1081344 | tf_op jit(solution)/shard_map/all_gather | solution.py:67
  9.8 52.8 %copy-start.13 = (bf16[512,1024]{1,0:T(8,128)(2,1)S(1)}, bf16[512,1024]{1,0:T(8,128)(2,1)}, u32[]{:S(2)}) copy-start(bf16[512,1024]{1,0:T(8,128)(2,1)} %param.12) | copy-start | bytes 3145732
  9.8 55.7 %all-to-all-start = ((bf16[32,16,1024]{2,1,0:T(8,128)(2,1)}), bf16[32,16,1024]{2,1,0:T(8,128)(2,1)S(1)}, u32[]{:S(2)}, u32[]{:S(2)}) async-start(bf16[32,16,1024]{2,1,0:T(8,128)(2,1)} %broadcast_in_dim.13), calls=%async_computation | async-start | bytes 2097152 | tf_op jit(solution)/shard_map/all_to_all | solution.py:52
  18.5 47.0 %copy-start.7 = (pred[64,8,4,256]{3,1,2,0:T(8,128)(4,1)}, pred[64,8,4,256]{3,1,2,0:T(8,128)(4,1)S(1)}, u32[]{:S(2)}) copy-start(pred[64,8,4,256]{3,1,2,0:T(8,128)(4,1)S(1)} %copy.29) | copy-start | bytes 1572868
  65.5 7.1 %slice-start.1 = ((s32[2048]{0:T(1024)}), s32[1024]{0:T(1024)S(1)}, s32[]{:S(2)}) async-start(s32[2048]{0:T(1024)} %param.13), calls=%async_computation.10 | async-start | bytes 8192 | tf_op jit(solution)/shard_map/slice | solution.py:14
  65.5 7.1 %slice-start.2 = ((s32[2048]{0:T(1024)}), s32[1024]{0:T(1024)S(1)}, s32[]{:S(2)}) async-start(s32[2048]{0:T(1024)} %param.14), calls=%async_computation.11 | async-start | bytes 8192 | tf_op jit(solution)/shard_map/slice | solution.py:14
  65.5 7.7 %copy-start.9 = (bf16[32,16,1024]{2,1,0:T(8,128)(2,1)}, bf16[32,16,1024]{2,1,0:T(8,128)(2,1)S(1)}, u32[]{:S(2)}) copy-start(bf16[32,16,1024]{2,1,0:T(8,128)(2,1)S(1)} %all-to-all-done) | copy-start | bytes 3145732
  65.5 36.2 %all-to-all-start.3 = ((f32[8,64,512]{2,1,0:T(8,128)}), f32[8,64,512]{2,1,0:T(8,128)S(1)}, u32[]{:S(2)}, u32[]{:S(2)}) async-start(f32[8,64,512]{2,1,0:T(8,128)} %bitcast.57), calls=%async_computation.4 | async-start | bytes 2097152 | tf_op jit(solution)/shard_map/all_to_all | solution.py:46
  73.5 7.5 %copy-start.5 = (pred[64,8,4,256]{3,1,2,0:T(8,128)(4,1)}, pred[64,8,4,256]{3,1,2,0:T(8,128)(4,1)S(1)}, u32[]{:S(2)}) copy-start(pred[64,8,4,256]{3,1,2,0:T(8,128)(4,1)S(1)} %copy.28) | copy-start | bytes 1572868
  75.2 5.8 %copy-start = (bf16[1024,512]{0,1:T(8,128)(2,1)}, bf16[1024,512]{0,1:T(8,128)(2,1)S(1)}, u32[]{:S(2)}) copy-start(bf16[1024,512]{0,1:T(8,128)(2,1)S(1)} %copy.23) | copy-start | bytes 3145732
  78.8 2.1 copy-start.10
  78.8 2.2 copy-start.12
  78.8 2.2 copy-start.15
  101.7 55.2 %all-to-all-start.1 = ((f32[8,64,1024]{2,1,0:T(8,128)}), f32[8,64,1024]{2,1,0:T(8,128)S(1)}, u32[]{:S(2)}, u32[]{:S(2)}) async-start(f32[8,64,1024]{2,1,0:T(8,128)} %bitcast.37), calls=%async_computation.1 | async-start | bytes 4194304 | tf_op jit(solution)/shard_map/all_to_all | solution.py:46
  158.0 24.2 %copy-start.8 = (pred[64,8,4,256]{3,1,2,0:T(8,128)(4,1)S(1)}, pred[64,8,4,256]{3,1,2,0:T(8,128)(4,1)}, u32[]{:S(2)}) copy-start(pred[64,8,4,256]{3,1,2,0:T(8,128)(4,1)} %copy-done.7) | copy-start | bytes 1572868
  158.0 24.2 %copy-start.14 = (bf16[512,1024]{1,0:T(8,128)(2,1)S(1)}, bf16[512,1024]{1,0:T(8,128)(2,1)}, u32[]{:S(2)}) copy-start(bf16[512,1024]{1,0:T(8,128)(2,1)} %param.12) | copy-start | bytes 3145732
  158.0 19.5 %all-to-all-start.2 = ((bf16[8,64,512]{2,1,0:T(8,128)(2,1)}), bf16[8,64,512]{2,1,0:T(8,128)(2,1)S(1)}, u32[]{:S(2)}, u32[]{:S(2)}) async-start(bf16[8,64,512]{2,1,0:T(8,128)(2,1)} %broadcast_in_dim.15), calls=%async_computation.2 | async-start | bytes 1048576 | tf_op jit(solution)/shard_map/all_to_all | solution.py:52
  178.6 29.9 %all-to-all-start.4 = ((bf16[8,64,1024]{2,1,0:T(8,128)(2,1)}), bf16[8,64,1024]{2,1,0:T(8,128)(2,1)S(1)}, u32[]{:S(2)}, u32[]{:S(2)}) async-start(bf16[8,64,1024]{2,1,0:T(8,128)(2,1)} %broadcast_in_dim.17), calls=%async_computation.5 | async-start | bytes 2097152 | tf_op jit(solution)/shard_map/all_to_all | solution.py:52
  182.2 91.5 %reduce-scatter.2.cloned.1.call-start = ((), (), s32[]{:S(2)}) async-start(), calls=%async_computation.7 | async-start | bytes 2162688 | tf_op jit(solution)/shard_map/reduce_scatter | solution.py:80
  184.3 24.2 %copy-start.16 = (pred[64,8,4,256]{3,1,2,0:T(8,128)(4,1)S(1)}, pred[64,8,4,256]{3,1,2,0:T(8,128)(4,1)}, u32[]{:S(2)}) copy-start(pred[64,8,4,256]{3,1,2,0:T(8,128)(4,1)} %copy.27) | copy-start | bytes 1572868
  208.5 2.4 copy-start.2
  208.5 2.4 copy-start.1
  208.5 2.4 copy-start.6
  213.0 35.6 %all-to-all-start.5 = ((f32[32,16,1024]{2,1,0:T(8,128)}), f32[32,16,1024]{2,1,0:T(8,128)S(1)}, u32[]{:S(2)}, u32[]{:S(2)}) async-start(f32[32,16,1024]{2,1,0:T(8,128)} %bitcast.8), calls=%async_computation.6 | async-start | bytes 4194304 | tf_op jit(solution)/shard_map/all_to_all | solution.py:46
  218.8 3.5 %copy-start.3 = (bf16[8,64,1024]{2,1,0:T(8,128)(2,1)S(1)}, bf16[8,64,1024]{2,1,0:T(8,128)(2,1)}, u32[]{:S(2)}) copy-start(bf16[8,64,1024]{2,1,0:T(8,128)(2,1)} %copy-done.2) | copy-start | bytes 3145732
  218.8 3.5 %copy-start.11 = (bf16[32,16,1024]{2,1,0:T(8,128)(2,1)S(1)}, bf16[32,16,1024]{2,1,0:T(8,128)(2,1)}, u32[]{:S(2)}) copy-start(bf16[32,16,1024]{2,1,0:T(8,128)(2,1)} %copy-done.9) | copy-start | bytes 3145732
  218.9 3.5 %copy-start.17 = (pred[64,8,4,256]{3,1,2,0:T(8,128)(4,1)S(1)}, pred[64,8,4,256]{3,1,2,0:T(8,128)(4,1)}, u32[]{:S(2)}) copy-start(pred[64,8,4,256]{3,1,2,0:T(8,128)(4,1)} %copy.27) | copy-start | bytes 1572868
  224.4 3.0 %copy-start.4 = (bf16[8,64,1024]{2,1,0:T(8,128)(2,1)S(1)}, bf16[8,64,1024]{2,1,0:T(8,128)(2,1)}, u32[]{:S(2)}) copy-start(bf16[8,64,1024]{2,1,0:T(8,128)(2,1)} %copy-done.2) | copy-start | bytes 3145732
Sparse Core Ops, SparseCore 0:
  10.5 51.9 all-gather.1
  186.8 86.8 reduce-scatter.1
where the time goes:
time: 283 us; the launch traced here: 282 us
  waiting for transfers between devices  193 us (68%)
  starting transfers between devices  31.5 us (11%)
  matrix products  21.3 us (8%)
  local copies, waits for them, and re-layouts  18.1 us (6%)
  between operations  14.4 us (5%)
  other arithmetic  3.28 us (1%)
    all_to_all x3, waiting for transfers between devices, a2a_scatter_sum(): return lax.all_to_all(pieces, axis_name, 0, 0, tiled=True).sum(axis=0)  84.3 us
    all_gather x1, waiting for transfers between devices, on_device(): cotangent_all = lax.all_gather(cotangent, 'col', axis=0, tiled=True)  44.1 us
    all_to_all x3, waiting for transfers between devices, a2a_gather(): gathered = lax.all_to_all(spread, axis_name, 0, 0, tiled=True)  40.1 us
    reduce_scatter x1, waiting for transfers between devices, on_device(): lax.psum_scatter(output_term, 'col', scatter_dimension=0, tiled=True)  24.4 us
    all_to_all x3, starting transfers between devices, a2a_scatter_sum(): return lax.all_to_all(pieces, axis_name, 0, 0, tiled=True).sum(axis=0)  16.5 us
    all_to_all x3, starting transfers between devices, a2a_gather(): gathered = lax.all_to_all(spread, axis_name, 0, 0, tiled=True)  14.9 us
    unnamed x43, local copies, waits for them, and re-layouts  11.4 us
    dot_general x3, matrix products, dense_apply(): lax.dot_general(left_operand, right_operand, (((0,), (0,)), ((), ())), pr...  8.97 us
  transfers between devices with their start and end apart: 8, of which 7 were waited for; matrix products, arithmetic and copies ran while one was open for 14% of the time, Pallas kernels for 0%

commit v1 on v0

--- a/solution.py
+++ b/solution.py
@@ -64,7 +64,9 @@
     keep_gate = kept_table(order_gate, row_start, col_start, rows_here, cols_here, hidden_blocks)
     keep_up = kept_table(order_up, row_start, col_start, rows_here, cols_here, hidden_blocks)
     keep_down = kept_table(order_down, col_start, row_start, cols_here, rows_here, width_blocks)
-    cotangent_all = lax.all_gather(cotangent, "col", axis=0, tiled=True)
+    cotangent_all = jnp.concatenate(
+        lax.all_to_all(jnp.stack([cotangent] * lax.axis_size("col")), "col", 0, 0), axis=0
+    )
     tokens_all = a2a_gather(tokens, "col")
     gate_term = apply_blocks(tokens_all, w_gate, keep_gate, "forward")
     up_term = apply_blocks(tokens_all, w_up, keep_up, "forward")

time: 283 us -> 273 us (0.965)
  waiting for transfers between devices: 193 us -> 162 us
  blocking collectives: 0 us -> 23.4 us
    all_gather x1 -> x0, waiting for transfers between devices: 44.1 us -> none  [on_device(): cotangent_all = lax.all_gather(cotangent, 'col', axis=0, tiled=True)]
    all_to_all x0 -> x1, blocking collectives: none -> 23.4 us  [on_device(): lax.all_to_all(jnp.stack([cotangent] * lax.axis_size('col')), 'col', 0, 0)]
    all_to_all x3, waiting for transfers between devices: 40.1 us -> 52.7 us  [a2a_gather(): gathered = lax.all_to_all(spread, axis_name, 0, 0, tiled=True)]
    unnamed x43 -> x49, local copies, waits for them, and re-layouts: 11.4 us -> 12 us
  transfers between devices with their start and end apart: 8 -> 7, of which waited for: 7 -> 7; matrix products, arithmetic and copies ran while one was open for 14% -> 13% of each run, Pallas kernels for 0% -> 0%
where the time goes in v1:
time: 273 us; the launch traced here: 272 us
  waiting for transfers between devices  162 us (59%)
  starting transfers between devices  29.6 us (11%)
  blocking collectives  23.4 us (9%)
  matrix products  20.2 us (7%)
  local copies, waits for them, and re-layouts  18.9 us (7%)
  between operations  14.4 us (5%)
  other arithmetic  3.28 us (1%)
    all_to_all x3, waiting for transfers between devices, a2a_scatter_sum(): return lax.all_to_all(pieces, axis_name, 0, 0, tiled=True).sum(axis=0)  85.3 us
    all_to_all x3, waiting for transfers between devices, a2a_gather(): gathered = lax.all_to_all(spread, axis_name, 0, 0, tiled=True)  52.7 us
    reduce_scatter x1, waiting for transfers between devices, on_device(): lax.psum_scatter(output_term, 'col', scatter_dimension=0, tiled=True)  24.4 us
    all_to_all x1, blocking collectives, on_device(): lax.all_to_all(jnp.stack([cotangent] * lax.axis_size('col')), 'col', 0, 0)  23.4 us
    all_to_all x3, starting transfers between devices, a2a_scatter_sum(): return lax.all_to_all(pieces, axis_name, 0, 0, tiled=True).sum(axis=0)  17.2 us
    all_to_all x3, starting transfers between devices, a2a_gather(): gathered = lax.all_to_all(spread, axis_name, 0, 0, tiled=True)  12.4 us
    unnamed x49, local copies, waits for them, and re-layouts  12 us
    dot_general x3, matrix products, dense_apply(): lax.dot_general(left_operand, right_operand, (((0,), (0,)), ((), ())), pr...  8.94 us
  transfers between devices with their start and end apart: 7, of which 7 were waited for; matrix products, arithmetic and copies ran while one was open for 13% of the time, Pallas kernels for 0%

profile of v1, /device:TPU:2, one launch (start us, length us, event | category | flops | bytes accessed | tf_op | source)
XLA Modules:
  0.0 272.1 jit_solution(6572268745190616335)
XLA Ops:
  8.1 23.4 %all_to_all.35 = bf16[32,16,1024]{2,1,0:T(8,128)(2,1)S(1)} all-to-all(bf16[32,16,1024]{2,1,0:T(8,128)(2,1)S(1)} %stack.2), channel_id=1, replica_groups=mesh['row'=8,'col'=32] {'col'}, dimensions={0} | all-to-all | bytes 2097152 | tf_op jit(solution)/shard_map/all_to_all | solution.py:68
  31.5 1.2 broadcast_in_dim.13
  32.7 5.2 %all-to-all-start = ((bf16[32,16,1024]{2,1,0:T(8,128)(2,1)}), bf16[32,16,1024]{2,1,0:T(8,128)(2,1)S(1)}, u32[]{:S(2)}, u32[]{:S(2)}) async-start(bf16[32,16,1024]{2,1,0:T(8,128)(2,1)} %broadcast_in_dim.13), calls=%async_computation | async-start | bytes 2097152 | tf_op jit(solution)/shard_map/all_to_all | solution.py:52
  39.6 1.7 fusion
  41.3 12.6 %all-to-all-done = bf16[32,16,1024]{2,1,0:T(8,128)(2,1)S(1)} async-done(((bf16[32,16,1024]{2,1,0:T(8,128)(2,1)}), bf16[32,16,1024]{2,1,0:T(8,128)(2,1)S(1)}, u32[]{:S(2)}, u32[]{:S(2)}) %all-to-all-start) | async-done | bytes 1048608 | tf_op jit(solution)/shard_map/all_to_all | solution.py:52
  54.0 1.0 copy-done.10
  54.9 8.5 %all-to-all-start.4 = ((f32[8,64,512]{2,1,0:T(8,128)}), f32[8,64,512]{2,1,0:T(8,128)S(1)}, u32[]{:S(2)}, u32[]{:S(2)}) async-start(f32[8,64,512]{2,1,0:T(8,128)} %bitcast.60), calls=%async_computation.5 | async-start | bytes 2097152 | tf_op jit(solution)/shard_map/all_to_all | solution.py:46
  64.1 1.1 copy.27
  65.8 1.3 copy.22
  67.1 1.5 copy.23
  68.6 2.4 convolution_bitcast_fusion
  72.0 1.8 copy.24
  73.8 18.8 %all-to-all-done.4 = f32[8,64,512]{2,1,0:T(8,128)S(1)} async-done(((f32[8,64,512]{2,1,0:T(8,128)}), f32[8,64,512]{2,1,0:T(8,128)S(1)}, u32[]{:S(2)}, u32[]{:S(2)}) %all-to-all-start.4) | async-done | bytes 1048608 | tf_op jit(solution)/shard_map/all_to_all | solution.py:46
  92.6 3.6 %all-to-all-start.1 = ((f32[8,64,1024]{2,1,0:T(8,128)}), f32[8,64,1024]{2,1,0:T(8,128)S(1)}, u32[]{:S(2)}, u32[]{:S(2)}) async-start(f32[8,64,1024]{2,1,0:T(8,128)} %bitcast.38), calls=%async_computation.1 | async-start | bytes 4194304 | tf_op jit(solution)/shard_map/all_to_all | solution.py:46
  96.3 51.5 %all-to-all-done.1 = f32[8,64,1024]{2,1,0:T(8,128)S(1)} async-done(((f32[8,64,1024]{2,1,0:T(8,128)}), f32[8,64,1024]{2,1,0:T(8,128)S(1)}, u32[]{:S(2)}, u32[]{:S(2)}) %all-to-all-start.1) | async-done | bytes 2097184 | tf_op jit(solution)/shard_map/all_to_all | solution.py:46
  148.9 3.6 %all-to-all-start.2 = ((bf16[8,64,512]{2,1,0:T(8,128)(2,1)}), bf16[8,64,512]{2,1,0:T(8,128)(2,1)S(1)}, u32[]{:S(2)}, u32[]{:S(2)}) async-start(bf16[8,64,512]{2,1,0:T(8,128)(2,1)} %broadcast_in_dim.15), calls=%async_computation.2 | async-start | bytes 1048576 | tf_op jit(solution)/shard_map/all_to_all | solution.py:52
  152.6 15.9 %all-to-all-done.2 = bf16[8,64,512]{2,1,0:T(8,128)(2,1)S(1)} async-done(((bf16[8,64,512]{2,1,0:T(8,128)(2,1)}), bf16[8,64,512]{2,1,0:T(8,128)(2,1)S(1)}, u32[]{:S(2)}, u32[]{:S(2)}) %all-to-all-start.2) | async-done | bytes 524320 | tf_op jit(solution)/shard_map/all_to_all | solution.py:52
  168.4 1.1 broadcast_in_dim.17
  169.5 3.6 %all-to-all-start.5 = ((bf16[8,64,1024]{2,1,0:T(8,128)(2,1)}), bf16[8,64,1024]{2,1,0:T(8,128)(2,1)S(1)}, u32[]{:S(2)}, u32[]{:S(2)}) async-start(bf16[8,64,1024]{2,1,0:T(8,128)(2,1)} %broadcast_in_dim.17), calls=%async_computation.6 | async-start | bytes 2097152 | tf_op jit(solution)/shard_map/all_to_all | solution.py:52
  173.1 2.1 fusion.2
  175.2 24.2 %all-to-all-done.5 = bf16[8,64,1024]{2,1,0:T(8,128)(2,1)S(1)} async-done(((bf16[8,64,1024]{2,1,0:T(8,128)(2,1)}), bf16[8,64,1024]{2,1,0:T(8,128)(2,1)S(1)}, u32[]{:S(2)}, u32[]{:S(2)}) %all-to-all-start.5) | async-done | bytes 1048608 | tf_op jit(solution)/shard_map/all_to_all | solution.py:52
  199.4 2.4 fusion.6
  201.8 2.0 convolution_add_fusion
  203.8 5.1 %all-to-all-start.6 = ((f32[32,16,1024]{2,1,0:T(8,128)}), f32[32,16,1024]{2,1,0:T(8,128)S(1)}, u32[]{:S(2)}, u32[]{:S(2)}) async-start(f32[32,16,1024]{2,1,0:T(8,128)} %bitcast.9), calls=%async_computation.7 | async-start | bytes 4194304 | tf_op jit(solution)/shard_map/all_to_all | solution.py:46
  209.0 3.4 %convolution_select_fusion = f32[512,1024]{1,0:T(8,128)} fusion(pred[512,1024]{1,0:T(8,128)(4,1)S(1)} %bitcast.53, bf16[512,512]{1,0:T(8,128)(2,1)S(1)} %bitcast.40, bf16[512,1024]{1,0:T(8,128)(2,1)} %bitcast.59), kind=kOutput, calls=%fused_computation.3 | convolution fusion | flops 537395200 | bytes 4194304 | tf_op jit(solution)/shard_map/dot_general | solution.py:33
  212.4 2.1 bitcast_select_fusion.1
  214.5 3.0 %copy.25 = f32[1024,512]{1,0:T(8,128)} copy(f32[1024,512]{0,1:T(8,128)} %bitcast_select_fusion.1) | data formatting | bytes 4194304
  217.5 3.4 %bitcast_select_fusion = f32[1024,512]{0,1:T(8,128)} fusion(pred[1024,512]{0,1:T(8,128)(4,1)} %bitcast.46, bf16[512,1024]{1,0:T(8,128)(2,1)} %bitcast.55, bf16[512,1024]{1,0:T(8,128)(2,1)S(1)} %bitcast.44), kind=kOutput, calls=%fused_computation.1 | convolution fusion | flops 537395200 | bytes 4194304 | tf_op jit(solution)/shard_map/dot_general | solution.py:33
  220.9 2.9 %copy.26 = f32[1024,512]{1,0:T(8,128)} copy(f32[1024,512]{0,1:T(8,128)} %bitcast_select_fusion) | data formatting | bytes 4194304
  223.8 14.9 %all-to-all-done.6 = f32[32,16,1024]{2,1,0:T(8,128)S(1)} async-done(((f32[32,16,1024]{2,1,0:T(8,128)}), f32[32,16,1024]{2,1,0:T(8,128)S(1)}, u32[]{:S(2)}, u32[]{:S(2)}) %all-to-all-start.6) | async-done | bytes 2097184 | tf_op jit(solution)/shard_map/all_to_all | solution.py:46
  239.4 24.4 %reduce-scatter.2.cloned.1.call-done = f32[16,1024]{1,0:T(8,128)} async-done(((f32[512,1024]{1,0:T(8,128)}), f32[16,1024]{1,0:T(8,128)}) %reduce-scatter.2.cloned.1.call-update) | async-done | bytes 65552 | tf_op jit(solution)/shard_map/reduce_scatter | solution.py:82
  263.8 1.5 convert_element_type.11
  (69 shorter events, 6.8 us)
Async XLA Ops:
  7.2 24.3 %copy-start.20 = (bf16[16,1024]{1,0:T(8,128)(2,1)S(1)}, bf16[16,1024]{1,0:T(8,128)(2,1)}, u32[]{:S(2)}) copy-start(bf16[16,1024]{1,0:T(8,128)(2,1)} %param.8) | copy-start | bytes 98308
  31.5 7.3 %copy-start.13 = (bf16[32,16,1024]{2,1,0:T(8,128)(2,1)}, bf16[32,16,1024]{2,1,0:T(8,128)(2,1)S(1)}, u32[]{:S(2)}) copy-start(bf16[32,16,1024]{2,1,0:T(8,128)(2,1)S(1)} %all_to_all.35) | copy-start | bytes 3145732
  31.5 6.5 %slice-start = ((s32[2048]{0:T(1024)}), s32[1024]{0:T(1024)S(1)}, s32[]{:S(2)}) async-start(s32[2048]{0:T(1024)} %param.15), calls=%async_computation.9 | async-start | bytes 8192 | tf_op jit(solution)/shard_map/slice | solution.py:14
  32.7 6.9 %copy-start.15 = (bf16[512,1024]{1,0:T(8,128)(2,1)S(1)}, bf16[512,1024]{1,0:T(8,128)(2,1)}, u32[]{:S(2)}) copy-start(bf16[512,1024]{1,0:T(8,128)(2,1)} %param.12) | copy-start | bytes 3145732
  32.7 21.3 %all-to-all-start = ((bf16[32,16,1024]{2,1,0:T(8,128)(2,1)}), bf16[32,16,1024]{2,1,0:T(8,128)(2,1)S(1)}, u32[]{:S(2)}, u32[]{:S(2)}) async-start(bf16[32,16,1024]{2,1,0:T(8,128)(2,1)} %broadcast_in_dim.13), calls=%async_computation | async-start | bytes 2097152 | tf_op jit(solution)/shard_map/all_to_all | solution.py:52
  38.8 0.8 copy-start.7
  41.3 22.2 %slice-start.1 = ((s32[2048]{0:T(1024)}), s32[1024]{0:T(1024)S(1)}, s32[]{:S(2)}) async-start(s32[2048]{0:T(1024)} %param.13), calls=%async_computation.10 | async-start | bytes 8192 | tf_op jit(solution)/shard_map/slice | solution.py:14
  41.3 22.2 %slice-start.2 = ((s32[2048]{0:T(1024)}), s32[1024]{0:T(1024)S(1)}, s32[]{:S(2)}) async-start(s32[2048]{0:T(1024)} %param.14), calls=%async_computation.11 | async-start | bytes 8192 | tf_op jit(solution)/shard_map/slice | solution.py:14
  54.0 1.0 copy-start.10
  54.9 37.7 %all-to-all-start.4 = ((f32[8,64,512]{2,1,0:T(8,128)}), f32[8,64,512]{2,1,0:T(8,128)S(1)}, u32[]{:S(2)}, u32[]{:S(2)}) async-start(f32[8,64,512]{2,1,0:T(8,128)} %bitcast.60), calls=%async_computation.5 | async-start | bytes 2097152 | tf_op jit(solution)/shard_map/all_to_all | solution.py:46
  63.4 2.3 copy-start.9
  65.7 5.2 %copy-start.5 = (pred[64,8,4,256]{3,1,2,0:T(8,128)(4,1)}, pred[64,8,4,256]{3,1,2,0:T(8,128)(4,1)S(1)}, u32[]{:S(2)}) copy-start(pred[64,8,4,256]{3,1,2,0:T(8,128)(4,1)S(1)} %copy.28) | copy-start | bytes 1572868
  68.6 2.4 copy-start
  68.6 2.4 copy-start.11
  68.6 2.4 copy-start.14
  68.6 2.4 copy-start.17
  92.6 55.2 %all-to-all-start.1 = ((f32[8,64,1024]{2,1,0:T(8,128)}), f32[8,64,1024]{2,1,0:T(8,128)S(1)}, u32[]{:S(2)}, u32[]{:S(2)}) async-start(f32[8,64,1024]{2,1,0:T(8,128)} %bitcast.38), calls=%async_computation.1 | async-start | bytes 4194304 | tf_op jit(solution)/shard_map/all_to_all | solution.py:46
  148.9 24.2 %copy-start.8 = (pred[64,8,4,256]{3,1,2,0:T(8,128)(4,1)S(1)}, pred[64,8,4,256]{3,1,2,0:T(8,128)(4,1)}, u32[]{:S(2)}) copy-start(pred[64,8,4,256]{3,1,2,0:T(8,128)(4,1)} %copy-done.7) | copy-start | bytes 1572868
  148.9 24.2 %copy-start.16 = (bf16[512,1024]{1,0:T(8,128)(2,1)S(1)}, bf16[512,1024]{1,0:T(8,128)(2,1)}, u32[]{:S(2)}) copy-start(bf16[512,1024]{1,0:T(8,128)(2,1)} %param.12) | copy-start | bytes 3145732
  148.9 19.5 %all-to-all-start.2 = ((bf16[8,64,512]{2,1,0:T(8,128)(2,1)}), bf16[8,64,512]{2,1,0:T(8,128)(2,1)S(1)}, u32[]{:S(2)}, u32[]{:S(2)}) async-start(bf16[8,64,512]{2,1,0:T(8,128)(2,1)} %broadcast_in_dim.15), calls=%async_computation.2 | async-start | bytes 1048576 | tf_op jit(solution)/shard_map/all_to_all | solution.py:52
  169.5 29.9 %all-to-all-start.5 = ((bf16[8,64,1024]{2,1,0:T(8,128)(2,1)}), bf16[8,64,1024]{2,1,0:T(8,128)(2,1)S(1)}, u32[]{:S(2)}, u32[]{:S(2)}) async-start(bf16[8,64,1024]{2,1,0:T(8,128)(2,1)} %broadcast_in_dim.17), calls=%async_computation.6 | async-start | bytes 2097152 | tf_op jit(solution)/shard_map/all_to_all | solution.py:52
  173.1 90.7 %reduce-scatter.2.cloned.1.call-start = ((), (), s32[]{:S(2)}) async-start(), calls=%async_computation.8 | async-start | bytes 2162688 | tf_op jit(solution)/shard_map/reduce_scatter | solution.py:82
  175.2 24.2 %copy-start.18 = (pred[64,8,4,256]{3,1,2,0:T(8,128)(4,1)S(1)}, pred[64,8,4,256]{3,1,2,0:T(8,128)(4,1)}, u32[]{:S(2)}) copy-start(pred[64,8,4,256]{3,1,2,0:T(8,128)(4,1)} %copy.27) | copy-start | bytes 1572868
  199.4 2.4 copy-start.2
  199.4 2.4 copy-start.1
  199.4 2.4 copy-start.6
  203.8 34.9 %all-to-all-start.6 = ((f32[32,16,1024]{2,1,0:T(8,128)}), f32[32,16,1024]{2,1,0:T(8,128)S(1)}, u32[]{:S(2)}, u32[]{:S(2)}) async-start(f32[32,16,1024]{2,1,0:T(8,128)} %bitcast.9), calls=%async_computation.7 | async-start | bytes 4194304 | tf_op jit(solution)/shard_map/all_to_all | solution.py:46
  208.9 3.5 %copy-start.3 = (bf16[8,64,1024]{2,1,0:T(8,128)(2,1)S(1)}, bf16[8,64,1024]{2,1,0:T(8,128)(2,1)}, u32[]{:S(2)}) copy-start(bf16[8,64,1024]{2,1,0:T(8,128)(2,1)} %copy-done.2) | copy-start | bytes 3145732
  209.0 3.5 %copy-start.12 = (bf16[32,16,1024]{2,1,0:T(8,128)(2,1)S(1)}, bf16[32,16,1024]{2,1,0:T(8,128)(2,1)}, u32[]{:S(2)}) copy-start(bf16[32,16,1024]{2,1,0:T(8,128)(2,1)} %copy-done.10) | copy-start | bytes 3145732
  209.0 3.5 %copy-start.19 = (pred[64,8,4,256]{3,1,2,0:T(8,128)(4,1)S(1)}, pred[64,8,4,256]{3,1,2,0:T(8,128)(4,1)}, u32[]{:S(2)}) copy-start(pred[64,8,4,256]{3,1,2,0:T(8,128)(4,1)} %copy.27) | copy-start | bytes 1572868
  214.5 3.0 %copy-start.4 = (bf16[8,64,1024]{2,1,0:T(8,128)(2,1)S(1)}, bf16[8,64,1024]{2,1,0:T(8,128)(2,1)}, u32[]{:S(2)}) copy-start(bf16[8,64,1024]{2,1,0:T(8,128)(2,1)} %copy-done.2) | copy-start | bytes 3145732
Sparse Core Ops, SparseCore 0:
  177.7 86.0 reduce-scatter.1
